TPU v7x, 128 devices: a whole 4x4x4 slice. The times are simulated.
128 devices in a mesh: req: 16 (over z, x), head: 8 (over y, core).
Axes of the slice: x: 4, y: 4, z: 4, core: 2. Of those that a mesh axis runs over, the one named last changes fastest.
Arguments:
- tokens: bfloat16 [256, 1280], P('req'), may hold values from -6 to 6
- w_qkv: bfloat16 [2, 3, 1280, 1280], P(None, None, 'head'), may hold values from -0.15625 to 0.15625
- w_out: bfloat16 [2, 1280, 1280], P(None, 'head'), may hold values from -0.15625 to 0.15625
- w_up: bfloat16 [2, 1280, 1280], P(None, 'head'), may hold values from -0.15625 to 0.15625
- w_down: bfloat16 [2, 1280, 1280], P(None, 'head'), may hold values from -0.15625 to 0.15625
- gain_attn: float32 [2, 1280], replicated, may hold values from 0.1 to 1.9
- gain_mlp: float32 [2, 1280], replicated, may hold values from 0.1 to 1.9
- suffix_cache: bfloat16 [2, 2, 512, 1280, 128], P(None, None, 'req', 'head'), may hold values from -110 to 110
- prompt_cache: bfloat16 [2, 2, 96, 1280, 128], P(None, None, 'req', 'head'), may hold values from -110 to 110
- suffix_table: int32 [16, 32], P('req'), may hold values from 0 to 31, each once within a row
- prompt_owner: int32 [96], replicated, may hold values from 0 to 95, each once
- suffix_len: int32 [256], P('req'), may hold values from 1 to 256, 32768 in all
- group_id: int32 [256], P('req'), may hold values from 0 to 23, never falling along the last dimension, each value on 1 to 16 neighbouring positions
Outputs:
- hidden: bfloat16 [256, 1280], P('req')
- new_cache: bfloat16 [2, 2, 256, 1280], P(None, None, 'req', 'head')
Inputs may be any that keep to these rules, and one draw needn't show every extreme that they name: `suffix_table`: each row holds every number once. `prompt_owner`: each number once. `group_id`: never falls from one request to the next; every group has 1 to 16 requests, one group exactly 16.
All inputs are finite; a program needn't handle non-finite values. No bound on the sum of `suffix_len` on one device may be relied on, other than what follows from the above.
Results may differ from a plain program's by a relative error of at most 0.019.
The roundings to bfloat16 on the way count: a program that leaves them out, or rounds other values in their place, can miss the bound.
Values may be sent and summed in bfloat16 or wider, within the bound.
No kernel may reach another device: no remote copies, remote signals or barrier semaphores. Data moves between devices by JAX's collectives and lax.ppermute only.
A program may use at most 128 MiB of HBM per device.

v0:
```python
import math
import jax
import jax.numpy as jnp
from jax import lax
from jax.sharding import PartitionSpec as P

HD = 80
PPAGES = 4
NEG_FLOOR = -1e30


def root_norm(values, gains):
    factor = lax.rsqrt(jnp.mean(values * values, axis=-1, keepdims=True) + 1e-06)
    return values * factor * gains


def page_groups(prompt_owner, count, page_len):
    owners = prompt_owner // PPAGES
    return jnp.repeat(owners, page_len, total_repeat_length=count * page_len)


def attend(
    query, key_new, val_new, layer_suffix, layer_prompt, pages, valid, group_id, prompt_owner
):
    row_count = query.shape[0]
    head_count = query.shape[1] // HD
    scale = 1.0 / math.sqrt(HD)
    page_len = layer_suffix.shape[3]
    own_pages = pages.shape[1]
    query_heads = query.reshape(row_count, head_count, HD)
    key_heads = key_new.reshape(row_count, head_count, HD)
    val_heads = val_new.reshape(row_count, head_count, HD)
    gathered_pages = layer_suffix[:, pages].reshape(
        2, row_count, own_pages, head_count, HD, page_len
    )
    scores = (
        jnp.einsum(
            "rhd,rphdt->rhpt", query_heads, gathered_pages[0], preferred_element_type=jnp.float32
        ).reshape(row_count, head_count, own_pages * page_len)
        * scale
    )
    own = (
        jnp.einsum("rhd,rhd->rh", query_heads, key_heads, preferred_element_type=jnp.float32)
        * scale
    )
    mask = valid[:, None, :]
    local_top = jnp.maximum(jnp.max(jnp.where(mask, scores, NEG_FLOOR), axis=-1), own)
    weights = jnp.exp(jnp.where(mask, scores - local_top[..., None], NEG_FLOOR))
    own_weight = jnp.exp(own - local_top)
    total = jnp.sum(weights, axis=-1) + own_weight
    weight_pages = weights.astype(jnp.bfloat16).reshape(row_count, head_count, own_pages, page_len)
    mixed = jnp.einsum(
        "rhpt,rphdt->rhd", weight_pages, gathered_pages[1], preferred_element_type=jnp.float32
    )
    mixed = mixed + jnp.einsum(
        "rh,rhd->rhd",
        own_weight.astype(jnp.bfloat16),
        val_heads,
        preferred_element_type=jnp.float32,
    )
    piece = lax.all_gather(layer_prompt, "req", axis=1, tiled=True)
    count = piece.shape[1]
    key_group = page_groups(prompt_owner, count, page_len)
    keys = piece[0].reshape(count, head_count, HD, page_len)
    vals = piece[1].reshape(count, head_count, HD, page_len)
    block = (
        jnp.einsum("rhd,phdt->rhpt", query_heads, keys, preferred_element_type=jnp.float32).reshape(
            row_count, head_count, count * page_len
        )
        * scale
    )
    match = (group_id[:, None] == key_group[None, :])[:, None, :]
    new_top = jnp.maximum(local_top, jnp.max(jnp.where(match, block, NEG_FLOOR), axis=-1))
    block_weights = jnp.exp(jnp.where(match, block - new_top[..., None], NEG_FLOOR))
    factor = jnp.exp(local_top - new_top)
    new_total = total * factor + jnp.sum(block_weights, axis=-1)
    block_rounded = block_weights.astype(jnp.bfloat16).reshape(
        row_count, head_count, count, page_len
    )
    new_mixed = mixed * factor[..., None] + jnp.einsum(
        "rhpt,phdt->rhd", block_rounded, vals, preferred_element_type=jnp.float32
    )
    return (new_mixed / new_total[..., None]).reshape(row_count, -1).astype(jnp.bfloat16)


def add_branch(residual, partial_value, gains, closing):
    residual = residual + lax.psum(partial_value, "head")
    if closing:
        normed = None
    else:
        normed = root_norm(residual, gains).astype(jnp.bfloat16)
    return (residual, normed)


def local(
    tokens,
    w_qkv,
    w_out,
    w_up,
    w_down,
    gain_attn,
    gain_mlp,
    suffix_cache,
    prompt_cache,
    suffix_table,
    prompt_owner,
    suffix_len,
    group_id,
):
    row_count = tokens.shape[0]
    layer_count = w_qkv.shape[0]
    width_here = w_qkv.shape[2]
    model_width = w_qkv.shape[3]
    pages = suffix_table[0].reshape(row_count, -1)
    span = pages.shape[1] * suffix_cache.shape[4]
    valid = jnp.arange(span, dtype=jnp.int32)[None, :] < suffix_len[:, None]
    whole = tokens.astype(jnp.float32)
    normed = root_norm(whole, gain_attn[0]).astype(jnp.bfloat16)
    residual = whole
    new_keys = []
    new_vals = []
    for layer in range(layer_count):
        projected = jnp.einsum(
            "rd,kd->rk",
            normed,
            w_qkv[layer].reshape(3 * width_here, model_width),
            preferred_element_type=jnp.float32,
        )
        projected = projected.reshape(row_count, 3, width_here).astype(jnp.bfloat16)
        query = projected[:, 0]
        key_new = projected[:, 1]
        val_new = projected[:, 2]
        new_keys.append(key_new)
        new_vals.append(val_new)
        attended = attend(
            query,
            key_new,
            val_new,
            suffix_cache[layer],
            prompt_cache[layer],
            pages,
            valid,
            group_id,
            prompt_owner,
        )
        partial_value = jnp.dot(attended, w_out[layer], preferred_element_type=jnp.float32)
        residual, normed = add_branch(residual, partial_value, gain_mlp[layer], False)
        hidden_units = jax.nn.silu(
            jnp.einsum("rd,fd->rf", normed, w_up[layer], preferred_element_type=jnp.float32)
        ).astype(jnp.bfloat16)
        partial_value = jnp.dot(hidden_units, w_down[layer], preferred_element_type=jnp.float32)
        closing = layer == layer_count - 1
        next_gains = gain_attn[layer] if closing else gain_attn[layer + 1]
        residual, normed = add_branch(residual, partial_value, next_gains, closing)
    hidden = residual.astype(jnp.bfloat16)
    new_cache = jnp.stack([jnp.stack(new_keys), jnp.stack(new_vals)], axis=1)
    return (hidden, new_cache)


def solution(mesh):
    placed = (
        P("req", None),
        P(None, None, "head", None),
        P(None, "head", None),
        P(None, "head", None),
        P(None, "head", None),
        P(),
        P(),
        P(None, None, "req", "head", None),
        P(None, None, "req", "head", None),
        P("req", None),
        P(),
        P("req"),
        P("req"),
    )
    return jax.shard_map(
        local,
        mesh=mesh,
        in_specs=placed,
        out_specs=(P("req", None), P(None, None, "req", "head")),
        check_vma=False,
    )
```

profile of v0, /device:TPU:1, one launch (start us, length us, event | category | flops | bytes accessed | tf_op | source)
XLA Modules:
  0.0 431.9 jit_solution(11187171101283764259)
XLA Ops:
  7.3 2.4 fusion.147
  11.4 0.7 reduce.26
  12.3 73.0 %gather_fusion.2 = s32[12288]{0:T(1024)S(1)} fusion(s32[96]{0:T(128)S(1)} %and_select_fusion, s32[12288]{0:T(1024)S(1)} %fusion.97), kind=kCustom, calls=%fused_computation.clone | custom fusion | bytes 147456 | tf_op jit(solution)/shard_map/jit(_take)/gather | solution.py:19
  85.4 4.6 %slice_bitcast_fusion = (bf16[2,32,160,128]{3,2,1,0:T(8,128)(2,1)S(1)}, bf16[2,32,160,128]{3,2,1,0:T(8,128)(2,1)}) fusion(bf16[2,2,32,160,128]{4,3,2,1,0:T(8,128)(2,1)} %param.26), kind=kLoop, calls=%fused_computation.11 | loop fusion | bytes 10485760 | tf_op jit(solution)/shard_map/squeeze | solution.py:139
  90.0 4.1 gather_fusion
  94.2 1.9 fusion.146
  97.3 3.6 fusion.144
  101.0 0.8 fusion.11
  102.3 1.2 fusion.62
  103.6 1.8 fusion.86
  105.5 0.7 all-gather.7.cloned.1.call-update
  106.3 2.4 gather_fusion.1
  108.8 3.0 fusion.145
  111.8 53.2 %all-reduce.5.cloned.1.call-done = f32[16,1280]{1,0:T(8,128)} async-done(((f32[16,1280]{1,0:T(8,128)}), f32[16,1280]{1,0:T(8,128)}) %all-reduce.5.cloned.1.call-update) | async-done | bytes 81936 | tf_op jit(solution)/shard_map/psum | solution.py:87
  165.0 1.0 multiply_reduce_fusion.2
  166.1 2.2 fusion.82
  168.3 67.2 %all-gather.7.cloned.1.call-done = bf16[1,2,96,160,128]{4,3,2,1,0:T(8,128)(2,1)} async-done(((bf16[1,2,6,160,128]{4,3,2,1,0:T(8,128)(2,1)}), bf16[1,2,96,160,128]{4,3,2,1,0:T(8,128)(2,1)}) %all-gather.7.cloned.1.call-update) | async-done | bytes 7864336 | tf_op jit(solution)/shard_map/all_gather | solution.py:61
  235.5 5.4 %fusion.143 = (bf16[1,1,96,160,128]{4,3,2,1,0:T(8,128)(2,1)}, bf16[1,1,96,160,128]{4,3,2,1,0:T(8,128)(2,1)}) fusion(bf16[1,2,96,160,128]{4,3,2,1,0:T(8,128)(2,1)} %all-gather.7.cloned.1.call-done), kind=kLoop, calls=%fused_computation.177 | loop fusion | bytes 15728640 | tf_op jit(solution)/shard_map/slice | solution.py:64
  241.0 52.7 %all-reduce.7.cloned.1.call-done = f32[16,1280]{1,0:T(8,128)} async-done(((f32[16,1280]{1,0:T(8,128)}), f32[16,1280]{1,0:T(8,128)}) %all-reduce.7.cloned.1.call-update) | async-done | bytes 81936 | tf_op jit(solution)/shard_map/psum | solution.py:87
  293.7 1.0 multiply_reduce_fusion.1
  294.7 1.7 fusion.41
  297.5 2.9 fusion.8
  300.4 1.7 fusion.20
  302.2 0.6 fusion.30
  302.7 3.3 fusion.65
  306.2 1.8 fusion.80
  308.1 56.1 %all-reduce.9.cloned.1.call-done = f32[16,1280]{1,0:T(8,128)} async-done(((f32[16,1280]{1,0:T(8,128)}), f32[16,1280]{1,0:T(8,128)}) %all-reduce.9.cloned.1.call-update) | async-done | bytes 81936 | tf_op jit(solution)/shard_map/psum | solution.py:87
  364.2 1.0 multiply_reduce_fusion
  365.2 2.2 fusion.76
  367.4 0.6 copy.45
  368.0 55.5 %all-reduce.11.cloned.1.call-done = f32[16,1280]{1,0:T(8,128)} async-done(((f32[16,1280]{1,0:T(8,128)}), f32[16,1280]{1,0:T(8,128)}) %all-reduce.11.cloned.1.call-update) | async-done | bytes 81936 | tf_op jit(solution)/shard_map/psum | solution.py:87
  423.5 1.5 add_convert_fusion
  (85 shorter events, 5.5 us)
Async XLA Ops:
  7.2 2.6 copy-start.4
  7.2 2.6 copy-start.2
  7.2 2.7 copy-start.3
  7.2 4.2 copy-start.8
  7.2 90.1 %all-gather.5.cloned.1.call-start = ((), (), s32[]{:S(2)}) async-start(), calls=%async_computation.4 | async-start | bytes 8355840 | tf_op jit(solution)/shard_map/all_gather | solution.py:61
  9.6 2.7 copy-start.9
  9.7 155.4 %all-reduce.5.cloned.1.call-start = ((), (), s32[]{:S(2)}) async-start(), calls=%async_computation | async-start | bytes 163840 | tf_op jit(solution)/shard_map/psum | solution.py:87
  90.0 4.2 copy-start.7
  94.2 2.5 copy-start.6
  105.5 130.1 %all-gather.7.cloned.1.call-start = ((), (), s32[]{:S(2)}) async-start(), calls=%async_computation.5 | async-start | bytes 8355840 | tf_op jit(solution)/shard_map/all_gather | solution.py:61
  106.2 187.5 %all-reduce.7.cloned.1.call-start = ((), (), s32[]{:S(2)}) async-start(), calls=%async_computation.1 | async-start | bytes 163840 | tf_op jit(solution)/shard_map/psum | solution.py:87
  106.2 2.5 copy-start.5
  108.7 57.3 %copy-start = (bf16[2,160,1280]{2,1,0:T(8,128)(2,1)S(1)}, bf16[2,160,1280]{2,1,0:T(8,128)(2,1)}, u32[]{:S(2)}) copy-start(bf16[2,160,1280]{2,1,0:T(8,128)(2,1)} %param.23) | copy-start | bytes 2457604
  168.3 125.4 %copy-start.1 = (f32[16,1280]{1,0:T(8,128)S(1)}, f32[16,1280]{1,0:T(8,128)}, u32[]{:S(2)}) copy-start(f32[16,1280]{1,0:T(8,128)} %all-reduce.5.cloned.1.call-done) | copy-start | bytes 245764
  168.3 195.9 %all-reduce.9.cloned.1.call-start = ((), (), s32[]{:S(2)}) async-start(), calls=%async_computation.2 | async-start | bytes 163840 | tf_op jit(solution)/shard_map/psum | solution.py:87
  308.0 115.5 %all-reduce.11.cloned.1.call-start = ((), (), s32[]{:S(2)}) async-start(), calls=%async_computation.3 | async-start | bytes 163840 | tf_op jit(solution)/shard_map/psum | solution.py:87
Sparse Core Ops, SparseCore 0:
  10.2 71.6 all-gather.4
  105.6 59.4 all-reduce.4
  167.2 68.3 all-gather.6
  237.7 55.9 all-reduce.6
  308.1 55.9 all-reduce.8
  367.5 55.9 all-reduce.10
where the time goes:
time: 433 us; the launch traced here: 432 us
  waiting for transfers between devices  286 us (66%)
  local copies, waits for them, and re-layouts  103 us (24%)
  matrix products  21.1 us (5%)
  between operations  14.4 us (3%)
  other arithmetic  7.59 us (2%)
    psum x4, waiting for transfers between devices, add_branch(): residual = residual + lax.psum(partial_value, 'head')  218 us
    gather x1, local copies, waits for them, and re-layouts, page_groups(): return jnp.repeat(owners, page_len, total_repeat_length=count * page_len)  73 us
    all_gather x2, waiting for transfers between devices, attend(): piece = lax.all_gather(layer_prompt, 'req', axis=1, tiled=True)  67.2 us
    slice x2, local copies, waits for them, and re-layouts, attend(): keys = piece[0].reshape(count, head_count, HD, page_len)  9.05 us
  transfers between devices with their start and end apart: 6, of which 5 were waited for; matrix products, arithmetic and copies ran while one was open for 24% of the time, Pallas kernels for 0%

commit v1 on v0

--- a/solution.py
+++ b/solution.py
@@ -1,3 +1,4 @@
+import functools
 import math
 import jax
 import jax.numpy as jnp
@@ -7,6 +8,27 @@
 HD = 80
 PPAGES = 4
 NEG_FLOOR = -1e30
+
+
+def _part_views(local_block, net_axis, ndim_at):
+    how_many = lax.axis_size(net_axis)
+    copies = [(s, (s + 1) % how_many) for s in range(how_many)]
+    gallery = [(s, (s - 1) % how_many) for s in range(how_many)]
+    heard, small = ([local_block], [local_block])
+    for _ in range(how_many // 2):
+        taken_in = lax.ppermute(heard[-1], net_axis, copies)
+        heard.append(taken_in)
+    for _ in range((how_many - 1) // 2):
+        top = lax.ppermute(small[-1], net_axis, gallery)
+        small.append(top)
+    met_up = jnp.concatenate([*heard[::-1], *small[1:]], axis=ndim_at)
+    mixed_arr = lax.axis_index(net_axis)
+    return jnp.roll(
+        met_up, shift=(mixed_arr - how_many // 2) * local_block.shape[ndim_at], axis=ndim_at
+    )
+
+
+state_widths_in = functools.partial(_part_views, net_axis="req", ndim_at=1)
 
 
 def root_norm(values, gains):
@@ -58,7 +80,7 @@
         val_heads,
         preferred_element_type=jnp.float32,
     )
-    piece = lax.all_gather(layer_prompt, "req", axis=1, tiled=True)
+    piece = state_widths_in(layer_prompt)
     count = piece.shape[1]
     key_group = page_groups(prompt_owner, count, page_len)
     keys = piece[0].reshape(count, head_count, HD, page_len)

time: 433 us -> 535 us (1.24)
  starting transfers between devices: 0.24 us -> 68.1 us
  local copies, waits for them, and re-layouts: 103 us -> 120 us
  other arithmetic: 7.59 us -> 16.2 us
  waiting for transfers between devices: 286 us -> 292 us
    ppermute x0 -> x30, starting transfers between devices: none -> 67.8 us  [the longest x14 63.9 us: _part_views(): top = lax.ppermute(small[-1], net_axis, gallery)]
    all_gather x2 -> x0, waiting for transfers between devices: 67.2 us -> none  [attend(): piece = lax.all_gather(layer_prompt, 'req', axis=1, tiled=True)]
    ppermute x0 -> x30, waiting for transfers between devices: none -> 64.2 us  [the longest x16 39.8 us: _part_views(): taken_in = lax.ppermute(heard[-1], net_axis, copies)]
    unnamed x22 -> x75, local copies, waits for them, and re-layouts: 1.18 us -> 20.8 us
    psum x4, waiting for transfers between devices: 218 us -> 228 us  [add_branch(): residual = residual + lax.psum(partial_value, 'head')]
    concatenate x0 -> x1, other arithmetic: none -> 7.07 us  [_part_views(): jnp.roll(met_up, shift=(mixed_arr - how_many // 2) * local_block.shape[nd...]
  transfers between devices with their start and end apart: 6 -> 34, of which waited for: 5 -> 18; matrix products, arithmetic and copies ran while one was open for 24% -> 23% of each run, Pallas kernels for 0% -> 0%
where the time goes in v1:
time: 535 us; the launch traced here: 534 us
  waiting for transfers between devices  292 us (55%)
  local copies, waits for them, and re-layouts  120 us (22%)
  starting transfers between devices  68.1 us (13%)
  matrix products  22.6 us (4%)
  other arithmetic  16.2 us (3%)
  between operations  14.3 us (3%)
    psum x4, waiting for transfers between devices, add_branch(): residual = residual + lax.psum(partial_value, 'head')  228 us
    gather x1, local copies, waits for them, and re-layouts, page_groups(): return jnp.repeat(owners, page_len, total_repeat_length=count * page_len)  73 us
    ppermute x14, starting transfers between devices, _part_views(): top = lax.ppermute(small[-1], net_axis, gallery)  63.9 us
    ppermute x16, waiting for transfers between devices, _part_views(): taken_in = lax.ppermute(heard[-1], net_axis, copies)  39.8 us
    ppermute x14, waiting for transfers between devices, _part_views(): top = lax.ppermute(small[-1], net_axis, gallery)  24.4 us
    unnamed x75, local copies, waits for them, and re-layouts  20.8 us
  transfers between devices with their start and end apart: 34, of which 18 were waited for; matrix products, arithmetic and copies ran while one was open for 23% of the time, Pallas kernels for 0%

profile of v1, /device:TPU:1, one launch (start us, length us, event | category | flops | bytes accessed | tf_op | source)
XLA Modules:
  0.0 533.8 jit_solution(5034129524176053934)
XLA Ops:
  11.5 4.7 collective-permute-start.8
  16.3 4.8 collective-permute-start.23
  29.7 8.4 %collective-permute-done.15 = bf16[2,6,160,128]{3,2,1,0:T(8,128)(2,1)} collective-permute-done((bf16[2,6,160,128]{3,2,1,0:T(8,128)(2,1)}, bf16[2,6,160,128]{3,2,1,0:T(8,128)(2,1)}, u32[]{:S(2)}, u32[]{:S(2)}) %collective-permute-start.15) | collective-permute-done | bytes 491552 | tf_op jit(solution)/shard_map/ppermute | solution.py:19
  38.0 10.5 %collective-permute-done.1 = bf16[2,6,160,128]{3,2,1,0:T(8,128)(2,1)} collective-permute-done((bf16[2,6,160,128]{3,2,1,0:T(8,128)(2,1)S(1)}, bf16[2,6,160,128]{3,2,1,0:T(8,128)(2,1)}, u32[]{:S(2)}, u32[]{:S(2)}) %collective-permute-start.1) | collective-permute-done | bytes 491552 | tf_op jit(solution)/shard_map/ppermute | solution.py:19
  48.6 4.5 slice_bitcast_fusion
  53.1 4.1 gather_fusion
  57.3 4.8 collective-permute-start.9
  63.5 6.1 %collective-permute-done.2 = bf16[2,6,160,128]{3,2,1,0:T(8,128)(2,1)} collective-permute-done((bf16[2,6,160,128]{3,2,1,0:T(8,128)(2,1)}, bf16[2,6,160,128]{3,2,1,0:T(8,128)(2,1)}, u32[]{:S(2)}, u32[]{:S(2)}) %collective-permute-start.2) | collective-permute-done | bytes 491552 | tf_op jit(solution)/shard_map/ppermute | solution.py:19
  72.9 4.8 collective-permute-start.10
  77.7 3.3 collective-permute-done.24
  81.0 5.5 %collective-permute-start.25 = (bf16[2,6,160,128]{3,2,1,0:T(8,128)(2,1)S(1)}, bf16[2,6,160,128]{3,2,1,0:T(8,128)(2,1)}, u32[]{:S(2)}, u32[]{:S(2)}) collective-permute-start(bf16[2,6,160,128]{3,2,1,0:T(8,128)(2,1)S(1)} %collective-permute-done.24), channel_id=1, source_target_pairs={{0,120},{8,0},{16,8},{24,16},{32,24},{40,32},{48,40},{56,48},{64,5... | collective-permute-start | bytes 1474568 | tf_op jit(solution)/shard_map/ppermute | solution.py:22
  86.6 3.8 collective-permute-done.3
  91.6 5.6 %collective-permute-start.11 = (bf16[2,6,160,128]{3,2,1,0:T(8,128)(2,1)}, bf16[2,6,160,128]{3,2,1,0:T(8,128)(2,1)}, u32[]{:S(2)}, u32[]{:S(2)}) collective-permute-start(bf16[2,6,160,128]{3,2,1,0:T(8,128)(2,1)} %collective-permute-done.10), channel_id=1, source_target_pairs={{0,120},{8,0},{16,8},{24,16},{32,24},{40,32},{48,40},{56,48},{64,5... | collective-permute-start | bytes 1474568 | tf_op jit(solution)/shard_map/ppermute | solution.py:22
  97.2 4.9 collective-permute-done.25
  102.1 5.6 %collective-permute-start.26 = (bf16[2,6,160,128]{3,2,1,0:T(8,128)(2,1)}, bf16[2,6,160,128]{3,2,1,0:T(8,128)(2,1)}, u32[]{:S(2)}, u32[]{:S(2)}) collective-permute-start(bf16[2,6,160,128]{3,2,1,0:T(8,128)(2,1)} %collective-permute-done.25), channel_id=1, source_target_pairs={{0,120},{8,0},{16,8},{24,16},{32,24},{40,32},{48,40},{56,48},{64,5... | collective-permute-start | bytes 1474568 | tf_op jit(solution)/shard_map/ppermute | solution.py:22
  108.1 4.6 collective-permute-done.11
  112.7 5.5 %collective-permute-start.12 = (bf16[2,6,160,128]{3,2,1,0:T(8,128)(2,1)}, bf16[2,6,160,128]{3,2,1,0:T(8,128)(2,1)}, u32[]{:S(2)}, u32[]{:S(2)}) collective-permute-start(bf16[2,6,160,128]{3,2,1,0:T(8,128)(2,1)} %collective-permute-done.11), channel_id=1, source_target_pairs={{0,120},{8,0},{16,8},{24,16},{32,24},{40,32},{48,40},{56,48},{64,5... | collective-permute-start | bytes 1474568 | tf_op jit(solution)/shard_map/ppermute | solution.py:22
  118.2 5.0 collective-permute-done.26
  123.3 5.5 %collective-permute-start.27 = (bf16[2,6,160,128]{3,2,1,0:T(8,128)(2,1)}, bf16[2,6,160,128]{3,2,1,0:T(8,128)(2,1)}, u32[]{:S(2)}, u32[]{:S(2)}) collective-permute-start(bf16[2,6,160,128]{3,2,1,0:T(8,128)(2,1)} %collective-permute-done.26), channel_id=1, source_target_pairs={{0,120},{8,0},{16,8},{24,16},{32,24},{40,32},{48,40},{56,48},{64,5... | collective-permute-start | bytes 1474568 | tf_op jit(solution)/shard_map/ppermute | solution.py:22
  131.5 73.0 %gather_fusion.2 = s32[12288]{0:T(1024)S(1)} fusion(s32[96]{0:T(128)S(1)} %and_select_fusion, s32[12288]{0:T(1024)S(1)} %fusion.71), kind=kCustom, calls=%fused_computation.clone | custom fusion | bytes 147456 | tf_op jit(solution)/shard_map/jit(_take)/gather | solution.py:41
  206.4 5.0 collective-permute-start.13
  217.5 5.1 collective-permute-start.14
  222.6 3.1 collective-permute-done.28
  225.7 5.4 %collective-permute-start.29 = (bf16[2,6,160,128]{3,2,1,0:T(8,128)(2,1)S(1)}, bf16[2,6,160,128]{3,2,1,0:T(8,128)(2,1)S(1)}, u32[]{:S(2)}, u32[]{:S(2)}) collective-permute-start(bf16[2,6,160,128]{3,2,1,0:T(8,128)(2,1)S(1)} %collective-permute-done.28), channel_id=1, source_target_pairs={{0,120},{8,0},{16,8},{24,16},{32,24},{40,32},{48,40},{56,48},{64,5... | collective-permute-start | bytes 1474568 | tf_op jit(solution)/shard_map/ppermute | solution.py:22
  237.9 7.1 %collective-permute-done.22 = bf16[2,6,160,128]{3,2,1,0:T(8,128)(2,1)S(1)} collective-permute-done((bf16[2,6,160,128]{3,2,1,0:T(8,128)(2,1)S(1)}, bf16[2,6,160,128]{3,2,1,0:T(8,128)(2,1)S(1)}, u32[]{:S(2)}, u32[]{:S(2)}) %collective-permute-start.22) | collective-permute-done | bytes 491552 | tf_op jit(solution)/shard_map/ppermute | solution.py:19
  259.2 7.1 %fusion = (bf16[2,96,160,128]{3,2,1,0:T(8,128)(2,1)}, bf16[2,96,160,128]{3,2,1,0:T(8,128)(2,1)S(1)}) fusion(s32[]{:T(128)S(6)} %select_n.90, bf16[2,96,160,128]{3,2,1,0:T(8,128)(2,1)S(1)} %constant_dynamic-update-slice_fusion.16, bf16[2,96,160,128]{3,2,1,0:T(8,128)(2,1)S(1)} %constant_dynamic-update-slice_fusion), kind=kLoop, calls=%fused_computation.7 | loop fusion | flops 7864320 | bytes 31457284 | tf_op jit(solution)/shard_map/jit(_roll_dynamic)/concatenate | solution.py:26
  270.5 66.0 %all-reduce.5.cloned.1.call-done = f32[16,1280]{1,0:T(8,128)} async-done(((f32[16,1280]{1,0:T(8,128)}), f32[16,1280]{1,0:T(8,128)}) %all-reduce.5.cloned.1.call-update) | async-done | bytes 81936 | tf_op jit(solution)/shard_map/psum | solution.py:109
  339.9 5.5 %fusion.115 = (bf16[1,96,160,128]{3,2,1,0:T(8,128)(2,1)}, bf16[1,96,160,128]{3,2,1,0:T(8,128)(2,1)}) fusion(bf16[2,96,160,128]{3,2,1,0:T(8,128)(2,1)} %get-tuple-element.82), kind=kLoop, calls=%fused_computation.207 | loop fusion | bytes 15728640 | tf_op jit(solution)/shard_map/slice | solution.py:86
  345.5 50.3 %all-reduce.7.cloned.1.call-done = f32[16,1280]{1,0:T(8,128)} async-done(((f32[16,1280]{1,0:T(8,128)}), f32[16,1280]{1,0:T(8,128)}) %all-reduce.7.cloned.1.call-update) | async-done | bytes 81936 | tf_op jit(solution)/shard_map/psum | solution.py:109
  404.9 3.3 fusion.47
  410.2 56.1 %all-reduce.9.cloned.1.call-done = f32[16,1280]{1,0:T(8,128)} async-done(((f32[16,1280]{1,0:T(8,128)}), f32[16,1280]{1,0:T(8,128)}) %all-reduce.9.cloned.1.call-update) | async-done | bytes 81936 | tf_op jit(solution)/shard_map/psum | solution.py:109
  470.3 55.5 %all-reduce.11.cloned.1.call-done = f32[16,1280]{1,0:T(8,128)} async-done(((f32[16,1280]{1,0:T(8,128)}), f32[16,1280]{1,0:T(8,128)}) %all-reduce.11.cloned.1.call-update) | async-done | bytes 81936 | tf_op jit(solution)/shard_map/psum | solution.py:109
  (196 shorter events, 74.6 us)
Async XLA Ops:
  7.2 329.4 %all-reduce.5.cloned.1.call-start = ((), (), s32[]{:S(2)}) async-start(), calls=%async_computation | async-start | bytes 163840 | tf_op jit(solution)/shard_map/psum | solution.py:109
  9.5 17.9 %collective-permute-start = (bf16[2,6,160,128]{3,2,1,0:T(8,128)(2,1)}, bf16[2,6,160,128]{3,2,1,0:T(8,128)(2,1)S(1)}, u32[]{:S(2)}, u32[]{:S(2)}) collective-permute-start(bf16[2,6,160,128]{3,2,1,0:T(8,128)(2,1)} %get-tuple-element.63), channel_id=1, source_target_pairs={{0,8},{8,16},{16,24},{24,32},{32,40},{40,48},{48,56},{56,64},{64,7... | collective-permute-start | bytes 1474568 | tf_op jit(solution)/shard_map/ppermute | solution.py:19
  11.5 45.8 %collective-permute-start.8 = (bf16[2,6,160,128]{3,2,1,0:T(8,128)(2,1)}, bf16[2,6,160,128]{3,2,1,0:T(8,128)(2,1)}, u32[]{:S(2)}, u32[]{:S(2)}) collective-permute-start(bf16[2,6,160,128]{3,2,1,0:T(8,128)(2,1)} %get-tuple-element.63), channel_id=1, source_target_pairs={{0,120},{8,0},{16,8},{24,16},{32,24},{40,32},{48,40},{56,48},{64,5... | collective-permute-start | bytes 1474568 | tf_op jit(solution)/shard_map/ppermute | solution.py:22
  16.3 21.8 %collective-permute-start.15 = (bf16[2,6,160,128]{3,2,1,0:T(8,128)(2,1)}, bf16[2,6,160,128]{3,2,1,0:T(8,128)(2,1)}, u32[]{:S(2)}, u32[]{:S(2)}) collective-permute-start(bf16[2,6,160,128]{3,2,1,0:T(8,128)(2,1)} %get-tuple-element.62), channel_id=1, source_target_pairs={{0,8},{8,16},{16,24},{24,32},{32,40},{40,48},{48,56},{56,64},{64,7... | collective-permute-start | bytes 1474568 | tf_op jit(solution)/shard_map/ppermute | solution.py:19
  16.3 45.8 %collective-permute-start.23 = (bf16[2,6,160,128]{3,2,1,0:T(8,128)(2,1)}, bf16[2,6,160,128]{3,2,1,0:T(8,128)(2,1)S(1)}, u32[]{:S(2)}, u32[]{:S(2)}) collective-permute-start(bf16[2,6,160,128]{3,2,1,0:T(8,128)(2,1)} %get-tuple-element.62), channel_id=1, source_target_pairs={{0,120},{8,0},{16,8},{24,16},{32,24},{40,32},{48,40},{56,48},{64,5... | collective-permute-start | bytes 1474568 | tf_op jit(solution)/shard_map/ppermute | solution.py:22
  27.4 21.2 %collective-permute-start.1 = (bf16[2,6,160,128]{3,2,1,0:T(8,128)(2,1)S(1)}, bf16[2,6,160,128]{3,2,1,0:T(8,128)(2,1)}, u32[]{:S(2)}, u32[]{:S(2)}) collective-permute-start(bf16[2,6,160,128]{3,2,1,0:T(8,128)(2,1)S(1)} %collective-permute-done), channel_id=1, source_target_pairs={{0,8},{8,16},{16,24},{24,32},{32,40},{40,48},{48,56},{56,64},{64,7... | collective-permute-start | bytes 1474568 | tf_op jit(solution)/shard_map/ppermute | solution.py:19
  38.0 24.1 %collective-permute-start.16 = (bf16[2,6,160,128]{3,2,1,0:T(8,128)(2,1)}, bf16[2,6,160,128]{3,2,1,0:T(8,128)(2,1)}, u32[]{:S(2)}, u32[]{:S(2)}) collective-permute-start(bf16[2,6,160,128]{3,2,1,0:T(8,128)(2,1)} %collective-permute-done.15), channel_id=1, source_target_pairs={{0,8},{8,16},{16,24},{24,32},{32,40},{40,48},{48,56},{56,64},{64,7... | collective-permute-start | bytes 1474568 | tf_op jit(solution)/shard_map/ppermute | solution.py:19
  48.6 21.1 %collective-permute-start.2 = (bf16[2,6,160,128]{3,2,1,0:T(8,128)(2,1)}, bf16[2,6,160,128]{3,2,1,0:T(8,128)(2,1)}, u32[]{:S(2)}, u32[]{:S(2)}) collective-permute-start(bf16[2,6,160,128]{3,2,1,0:T(8,128)(2,1)} %collective-permute-done.1), channel_id=1, source_target_pairs={{0,8},{8,16},{16,24},{24,32},{32,40},{40,48},{48,56},{56,64},{64,7... | collective-permute-start | bytes 1474568 | tf_op jit(solution)/shard_map/ppermute | solution.py:19
  57.3 15.6 %collective-permute-start.9 = (bf16[2,6,160,128]{3,2,1,0:T(8,128)(2,1)}, bf16[2,6,160,128]{3,2,1,0:T(8,128)(2,1)S(1)}, u32[]{:S(2)}, u32[]{:S(2)}) collective-permute-start(bf16[2,6,160,128]{3,2,1,0:T(8,128)(2,1)} %collective-permute-done.8), channel_id=1, source_target_pairs={{0,120},{8,0},{16,8},{24,16},{32,24},{40,32},{48,40},{56,48},{64,5... | collective-permute-start | bytes 1474568 | tf_op jit(solution)/shard_map/ppermute | solution.py:22
  62.1 18.9 %collective-permute-start.24 = (bf16[2,6,160,128]{3,2,1,0:T(8,128)(2,1)S(1)}, bf16[2,6,160,128]{3,2,1,0:T(8,128)(2,1)S(1)}, u32[]{:S(2)}, u32[]{:S(2)}) collective-permute-start(bf16[2,6,160,128]{3,2,1,0:T(8,128)(2,1)S(1)} %collective-permute-done.23), channel_id=1, source_target_pairs={{0,120},{8,0},{16,8},{24,16},{32,24},{40,32},{48,40},{56,48},{64,5... | collective-permute-start | bytes 1474568 | tf_op jit(solution)/shard_map/ppermute | solution.py:22
  62.2 24.4 %collective-permute-start.17 = (bf16[2,6,160,128]{3,2,1,0:T(8,128)(2,1)}, bf16[2,6,160,128]{3,2,1,0:T(8,128)(2,1)S(1)}, u32[]{:S(2)}, u32[]{:S(2)}) collective-permute-start(bf16[2,6,160,128]{3,2,1,0:T(8,128)(2,1)} %collective-permute-done.16), channel_id=1, source_target_pairs={{0,8},{8,16},{16,24},{24,32},{32,40},{40,48},{48,56},{56,64},{64,7... | collective-permute-start | bytes 1474568 | tf_op jit(solution)/shard_map/ppermute | solution.py:19
  69.6 20.7 %collective-permute-start.3 = (bf16[2,6,160,128]{3,2,1,0:T(8,128)(2,1)}, bf16[2,6,160,128]{3,2,1,0:T(8,128)(2,1)S(1)}, u32[]{:S(2)}, u32[]{:S(2)}) collective-permute-start(bf16[2,6,160,128]{3,2,1,0:T(8,128)(2,1)} %collective-permute-done.2), channel_id=1, source_target_pairs={{0,8},{8,16},{16,24},{24,32},{32,40},{40,48},{48,56},{56,64},{64,7... | collective-permute-start | bytes 1474568 | tf_op jit(solution)/shard_map/ppermute | solution.py:19
  72.9 18.7 %collective-permute-start.10 = (bf16[2,6,160,128]{3,2,1,0:T(8,128)(2,1)S(1)}, bf16[2,6,160,128]{3,2,1,0:T(8,128)(2,1)}, u32[]{:S(2)}, u32[]{:S(2)}) collective-permute-start(bf16[2,6,160,128]{3,2,1,0:T(8,128)(2,1)S(1)} %collective-permute-done.9), channel_id=1, source_target_pairs={{0,120},{8,0},{16,8},{24,16},{32,24},{40,32},{48,40},{56,48},{64,5... | collective-permute-start | bytes 1474568 | tf_op jit(solution)/shard_map/ppermute | solution.py:22
  81.0 21.1 %collective-permute-start.25 = (bf16[2,6,160,128]{3,2,1,0:T(8,128)(2,1)S(1)}, bf16[2,6,160,128]{3,2,1,0:T(8,128)(2,1)}, u32[]{:S(2)}, u32[]{:S(2)}) collective-permute-start(bf16[2,6,160,128]{3,2,1,0:T(8,128)(2,1)S(1)} %collective-permute-done.24), channel_id=1, source_target_pairs={{0,120},{8,0},{16,8},{24,16},{32,24},{40,32},{48,40},{56,48},{64,5... | collective-permute-start | bytes 1474568 | tf_op jit(solution)/shard_map/ppermute | solution.py:22
  86.5 21.2 %collective-permute-start.18 = (bf16[2,6,160,128]{3,2,1,0:T(8,128)(2,1)S(1)}, bf16[2,6,160,128]{3,2,1,0:T(8,128)(2,1)}, u32[]{:S(2)}, u32[]{:S(2)}) collective-permute-start(bf16[2,6,160,128]{3,2,1,0:T(8,128)(2,1)S(1)} %collective-permute-done.17), channel_id=1, source_target_pairs={{0,8},{8,16},{16,24},{24,32},{32,40},{40,48},{48,56},{56,64},{64,7... | collective-permute-start | bytes 1474568 | tf_op jit(solution)/shard_map/ppermute | solution.py:19
  90.3 17.5 %collective-permute-start.4 = (bf16[2,6,160,128]{3,2,1,0:T(8,128)(2,1)S(1)}, bf16[2,6,160,128]{3,2,1,0:T(8,128)(2,1)}, u32[]{:S(2)}, u32[]{:S(2)}) collective-permute-start(bf16[2,6,160,128]{3,2,1,0:T(8,128)(2,1)S(1)} %collective-permute-done.3), channel_id=1, source_target_pairs={{0,8},{8,16},{16,24},{24,32},{32,40},{40,48},{48,56},{56,64},{64,7... | collective-permute-start | bytes 1474568 | tf_op jit(solution)/shard_map/ppermute | solution.py:19
  91.6 21.2 %collective-permute-start.11 = (bf16[2,6,160,128]{3,2,1,0:T(8,128)(2,1)}, bf16[2,6,160,128]{3,2,1,0:T(8,128)(2,1)}, u32[]{:S(2)}, u32[]{:S(2)}) collective-permute-start(bf16[2,6,160,128]{3,2,1,0:T(8,128)(2,1)} %collective-permute-done.10), channel_id=1, source_target_pairs={{0,120},{8,0},{16,8},{24,16},{32,24},{40,32},{48,40},{56,48},{64,5... | collective-permute-start | bytes 1474568 | tf_op jit(solution)/shard_map/ppermute | solution.py:22
  102.1 21.2 %collective-permute-start.26 = (bf16[2,6,160,128]{3,2,1,0:T(8,128)(2,1)}, bf16[2,6,160,128]{3,2,1,0:T(8,128)(2,1)}, u32[]{:S(2)}, u32[]{:S(2)}) collective-permute-start(bf16[2,6,160,128]{3,2,1,0:T(8,128)(2,1)} %collective-permute-done.25), channel_id=1, source_target_pairs={{0,120},{8,0},{16,8},{24,16},{32,24},{40,32},{48,40},{56,48},{64,5... | collective-permute-start | bytes 1474568 | tf_op jit(solution)/shard_map/ppermute | solution.py:22
  107.7 21.1 %collective-permute-start.19 = (bf16[2,6,160,128]{3,2,1,0:T(8,128)(2,1)}, bf16[2,6,160,128]{3,2,1,0:T(8,128)(2,1)}, u32[]{:S(2)}, u32[]{:S(2)}) collective-permute-start(bf16[2,6,160,128]{3,2,1,0:T(8,128)(2,1)} %collective-permute-done.18), channel_id=1, source_target_pairs={{0,8},{8,16},{16,24},{24,32},{32,40},{40,48},{48,56},{56,64},{64,7... | collective-permute-start | bytes 1474568 | tf_op jit(solution)/shard_map/ppermute | solution.py:19
  107.8 21.0 %collective-permute-start.5 = (bf16[2,6,160,128]{3,2,1,0:T(8,128)(2,1)}, bf16[2,6,160,128]{3,2,1,0:T(8,128)(2,1)}, u32[]{:S(2)}, u32[]{:S(2)}) collective-permute-start(bf16[2,6,160,128]{3,2,1,0:T(8,128)(2,1)} %collective-permute-done.4), channel_id=1, source_target_pairs={{0,8},{8,16},{16,24},{24,32},{32,40},{40,48},{48,56},{56,64},{64,7... | collective-permute-start | bytes 1474568 | tf_op jit(solution)/shard_map/ppermute | solution.py:19
  112.7 93.7 %collective-permute-start.12 = (bf16[2,6,160,128]{3,2,1,0:T(8,128)(2,1)}, bf16[2,6,160,128]{3,2,1,0:T(8,128)(2,1)}, u32[]{:S(2)}, u32[]{:S(2)}) collective-permute-start(bf16[2,6,160,128]{3,2,1,0:T(8,128)(2,1)} %collective-permute-done.11), channel_id=1, source_target_pairs={{0,120},{8,0},{16,8},{24,16},{32,24},{40,32},{48,40},{56,48},{64,5... | collective-permute-start | bytes 1474568 | tf_op jit(solution)/shard_map/ppermute | solution.py:22
  123.3 88.1 %collective-permute-start.27 = (bf16[2,6,160,128]{3,2,1,0:T(8,128)(2,1)}, bf16[2,6,160,128]{3,2,1,0:T(8,128)(2,1)}, u32[]{:S(2)}, u32[]{:S(2)}) collective-permute-start(bf16[2,6,160,128]{3,2,1,0:T(8,128)(2,1)} %collective-permute-done.26), channel_id=1, source_target_pairs={{0,120},{8,0},{16,8},{24,16},{32,24},{40,32},{48,40},{56,48},{64,5... | collective-permute-start | bytes 1474568 | tf_op jit(solution)/shard_map/ppermute | solution.py:22
  128.8 84.0 %collective-permute-start.20 = (bf16[2,6,160,128]{3,2,1,0:T(8,128)(2,1)}, bf16[2,6,160,128]{3,2,1,0:T(8,128)(2,1)}, u32[]{:S(2)}, u32[]{:S(2)}) collective-permute-start(bf16[2,6,160,128]{3,2,1,0:T(8,128)(2,1)} %collective-permute-done.19), channel_id=1, source_target_pairs={{0,8},{8,16},{16,24},{24,32},{32,40},{40,48},{48,56},{56,64},{64,7... | collective-permute-start | bytes 1474568 | tf_op jit(solution)/shard_map/ppermute | solution.py:19
  128.8 84.1 %collective-permute-start.6 = (bf16[2,6,160,128]{3,2,1,0:T(8,128)(2,1)}, bf16[2,6,160,128]{3,2,1,0:T(8,128)(2,1)}, u32[]{:S(2)}, u32[]{:S(2)}) collective-permute-start(bf16[2,6,160,128]{3,2,1,0:T(8,128)(2,1)} %collective-permute-done.5), channel_id=1, source_target_pairs={{0,8},{8,16},{16,24},{24,32},{32,40},{40,48},{48,56},{56,64},{64,7... | collective-permute-start | bytes 1474568 | tf_op jit(solution)/shard_map/ppermute | solution.py:19
  211.4 14.3 %collective-permute-start.28 = (bf16[2,6,160,128]{3,2,1,0:T(8,128)(2,1)}, bf16[2,6,160,128]{3,2,1,0:T(8,128)(2,1)S(1)}, u32[]{:S(2)}, u32[]{:S(2)}) collective-permute-start(bf16[2,6,160,128]{3,2,1,0:T(8,128)(2,1)} %collective-permute-done.27), channel_id=1, source_target_pairs={{0,120},{8,0},{16,8},{24,16},{32,24},{40,32},{48,40},{56,48},{64,5... | collective-permute-start | bytes 1474568 | tf_op jit(solution)/shard_map/ppermute | solution.py:22
  212.8 18.3 %collective-permute-start.21 = (bf16[2,6,160,128]{3,2,1,0:T(8,128)(2,1)}, bf16[2,6,160,128]{3,2,1,0:T(8,128)(2,1)S(1)}, u32[]{:S(2)}, u32[]{:S(2)}) collective-permute-start(bf16[2,6,160,128]{3,2,1,0:T(8,128)(2,1)} %collective-permute-done.20), channel_id=1, source_target_pairs={{0,8},{8,16},{16,24},{24,32},{32,40},{40,48},{48,56},{56,64},{64,7... | collective-permute-start | bytes 1474568 | tf_op jit(solution)/shard_map/ppermute | solution.py:19
  212.8 19.3 %collective-permute-start.7 = (bf16[2,6,160,128]{3,2,1,0:T(8,128)(2,1)}, bf16[2,6,160,128]{3,2,1,0:T(8,128)(2,1)S(1)}, u32[]{:S(2)}, u32[]{:S(2)}) collective-permute-start(bf16[2,6,160,128]{3,2,1,0:T(8,128)(2,1)} %collective-permute-done.6), channel_id=1, source_target_pairs={{0,8},{8,16},{16,24},{24,32},{32,40},{40,48},{48,56},{56,64},{64,7... | collective-permute-start | bytes 1474568 | tf_op jit(solution)/shard_map/ppermute | solution.py:19
  217.5 41.6 %collective-permute-start.14 = (bf16[2,6,160,128]{3,2,1,0:T(8,128)(2,1)S(1)}, bf16[2,6,160,128]{3,2,1,0:T(8,128)(2,1)S(1)}, u32[]{:S(2)}, u32[]{:S(2)}) collective-permute-start(bf16[2,6,160,128]{3,2,1,0:T(8,128)(2,1)S(1)} %collective-permute-done.13), channel_id=1, source_target_pairs={{0,120},{8,0},{16,8},{24,16},{32,24},{40,32},{48,40},{56,48},{64,5... | collective-permute-start | bytes 1474568 | tf_op jit(solution)/shard_map/ppermute | solution.py:22
  225.7 33.4 %collective-permute-start.29 = (bf16[2,6,160,128]{3,2,1,0:T(8,128)(2,1)S(1)}, bf16[2,6,160,128]{3,2,1,0:T(8,128)(2,1)S(1)}, u32[]{:S(2)}, u32[]{:S(2)}) collective-permute-start(bf16[2,6,160,128]{3,2,1,0:T(8,128)(2,1)S(1)} %collective-permute-done.28), channel_id=1, source_target_pairs={{0,120},{8,0},{16,8},{24,16},{32,24},{40,32},{48,40},{56,48},{64,5... | collective-permute-start | bytes 1474568 | tf_op jit(solution)/shard_map/ppermute | solution.py:22
  270.4 125.4 %all-reduce.7.cloned.1.call-start = ((), (), s32[]{:S(2)}) async-start(), calls=%async_computation.1 | async-start | bytes 163840 | tf_op jit(solution)/shard_map/psum | solution.py:109
  339.6 126.7 %all-reduce.9.cloned.1.call-start = ((), (), s32[]{:S(2)}) async-start(), calls=%async_computation.2 | async-start | bytes 163840 | tf_op jit(solution)/shard_map/psum | solution.py:109
  410.1 115.6 %all-reduce.11.cloned.1.call-start = ((), (), s32[]{:S(2)}) async-start(), calls=%async_computation.3 | async-start | bytes 163840 | tf_op jit(solution)/shard_map/psum | solution.py:109
  (24 other events, 856.8 us)
Sparse Core Ops, SparseCore 0:
  270.5 65.9 all-reduce.4
  339.8 55.9 all-reduce.6
  410.3 55.9 all-reduce.8
  469.7 55.9 all-reduce.10
